TPU v7x, 128 devices: a whole 4x4x4 slice. The times are simulated.
128 devices in a mesh: req: 8 (over y, core), hid: 16 (over x, z).
Axes of the slice: x: 4, y: 4, z: 4, core: 2. Of those that a mesh axis runs over, the one named last changes fastest.
Arguments:
- tokens: bfloat16 [24576, 1536], P(('req', 'hid')), may hold values from -6 to 6
- segment: int32 [24576], P(('req', 'hid')), may hold values from 0 to 35, as said below
- attn_gain: float32 [1536], replicated, may hold values from 0.1 to 1.9
- w_query: bfloat16 [1536, 1536], replicated, may hold values from -0.2 to 0.2
- w_key: bfloat16 [1536, 512], replicated, may hold values from -0.2 to 0.2
- w_value: bfloat16 [1536, 512], replicated, may hold values from -0.15625 to 0.15625
- q_gain: float32 [64], replicated, may hold values from 0.5 to 6
- k_gain: float32 [64], replicated, may hold values from 0.5 to 6
- w_out: bfloat16 [1536, 1536], replicated, may hold values from -0.15625 to 0.15625
- ffn_gain: float32 [1536], replicated, may hold values from 0.1 to 1.9
- w_gate: bfloat16 [4608, 1536], P(('req', 'hid')), may hold values from -0.15625 to 0.15625
- w_up: bfloat16 [4608, 1536], P(('req', 'hid')), may hold values from -0.15625 to 0.15625
- w_down: bfloat16 [4608, 1536], P(('req', 'hid')), may hold values from -0.09375 to 0.09375
Outputs:
- mixed: bfloat16 [24576, 1536], P(('req', 'hid'))
- kv_cache: bfloat16 [24576, 1024], P(('req', 'hid'))
Inputs may be any that keep to these rules, and one draw needn't show every extreme that they name: Segment ids never fall along the tokens and start at 0. A segment never crosses a boundary between aligned blocks of 3072 tokens; the first block is one segment of exactly 3072 tokens, and every later block holds exactly five segments.
All inputs are finite; a program needn't handle non-finite values.
Results may differ from a plain program's by a relative error of at most 0.015.
Values may be sent and summed in bfloat16 or wider, within the bound.
No kernel may reach another device: no remote copies, remote signals or barrier semaphores. Data moves between devices by JAX's collectives and lax.ppermute only.
A program may use at most 128 MiB of HBM per device.

v0:
```python
import jax
import jax.numpy as jnp
from jax import lax
from jax.sharding import PartitionSpec as P

H = 24
KVH = 8
HD = 64
EPSILON = 1e-05
ROPE_BASE = 1000000.0
NEG_FILL = -1e30
SCORE_SCALE = 0.125


def rms_scale(values, gain):
    mean_sq = jnp.mean(values * values, axis=-1, keepdims=True)
    return values * lax.rsqrt(mean_sq + EPSILON) * gain


def seg_positions(seg_ids):
    indices = jnp.arange(seg_ids.shape[0], dtype=jnp.int32)
    is_first = jnp.concatenate([jnp.ones((1,), bool), seg_ids[1:] != seg_ids[:-1]])
    seg_begin = lax.cummax(jnp.where(is_first, indices, jnp.zeros_like(indices)), axis=0)
    return indices - seg_begin


def rotate(heads, positions):
    half_dim = heads.shape[-1] // 2
    inv_freq = ROPE_BASE ** (-(jnp.arange(half_dim, dtype=jnp.float32) * 2.0) / (2.0 * half_dim))
    angles = positions.astype(jnp.float32)[:, None] * inv_freq[None, :]
    cos_val = jnp.cos(angles)[:, None, :]
    sin_val = jnp.sin(angles)[:, None, :]
    left = heads[..., :half_dim]
    right = heads[..., half_dim:]
    return jnp.concatenate(
        [left * cos_val - right * sin_val, right * cos_val + left * sin_val], axis=-1
    )


def block_length(shard_rows):
    return 4 * shard_rows


def key_block(running, key_blk, val_blk, key_idx, q_grid, seg_start, query_idx):
    run_peak, run_total, run_acc = running
    k_grid = key_blk.reshape(-1, KVH, HD).transpose(1, 0, 2)
    v_grid = val_blk.reshape(-1, KVH, HD).transpose(1, 0, 2)
    scores = (
        jnp.einsum("kgqd,kcd->kgqc", q_grid, k_grid, preferred_element_type=jnp.float32)
        * SCORE_SCALE
    )
    allowed = (key_idx[None, :] <= query_idx[:, None]) & (key_idx[None, :] >= seg_start[:, None])
    scores = jnp.where(allowed, scores, NEG_FILL)
    new_peak = jnp.maximum(run_peak, jnp.max(scores, axis=-1))
    weights = jnp.where(allowed, jnp.exp(scores - new_peak[..., None]), 0.0)
    factor = jnp.exp(run_peak - new_peak)
    new_total = run_total * factor + jnp.sum(weights, axis=-1)
    product = jnp.einsum(
        "kgqc,kcd->kgqd", weights.astype(jnp.bfloat16), v_grid, preferred_element_type=jnp.float32
    )
    return (new_peak, new_total, run_acc * factor[..., None] + product)


def unit_terms(pieces, gathered):
    gate_part, up_part, down_part = pieces
    contract = (((1,), (1,)), ((), ()))
    gate_act = lax.dot_general(gathered, gate_part, contract, preferred_element_type=jnp.float32)
    up_act = lax.dot_general(gathered, up_part, contract, preferred_element_type=jnp.float32)
    hidden = (jax.nn.silu(gate_act) * up_act).astype(jnp.bfloat16)
    return jnp.dot(hidden, down_part, preferred_element_type=jnp.float32)


def join_runs(left, right):
    l_last, l_trail, l_full = left
    r_last, r_trail, r_full = right
    same = (l_last == r_last) & (r_full > 0)
    trail = r_trail + jnp.where(same, l_trail, 0)
    full = jnp.where(same & (l_full > 0), 1, 0)
    return (r_last, trail, full)


def group_positions(seg_ids, axis):
    count = lax.psum(1, axis)
    me = lax.axis_index(axis)
    rows = seg_ids.shape[0]
    last = seg_ids[rows - 1]
    trail = jnp.sum((seg_ids == last).astype(jnp.int32))
    full = (seg_ids[0] == last).astype(jnp.int32)
    summary = jnp.stack([last, trail, full])
    shift = 1
    while shift < count:
        pairs = [(src, src + shift) for src in range(count - shift)]
        got = lax.ppermute(summary, axis, pairs)
        joined = jnp.stack(
            join_runs((got[0], got[1], got[2]), (summary[0], summary[1], summary[2]))
        )
        summary = jnp.where(me >= shift, joined, summary)
        shift *= 2
    before = lax.ppermute(summary, axis, [(src, src + 1) for src in range(count - 1)])
    local = seg_positions(seg_ids)
    lead = local == jnp.arange(rows, dtype=jnp.int32)
    carry = jnp.where((me > 0) & (before[0] == seg_ids[0]), before[1], 0)
    return local + jnp.where(lead, carry, 0)


def per_device(
    tokens,
    segment,
    attn_gain,
    w_query,
    w_key,
    w_value,
    q_gain,
    k_gain,
    w_out,
    ffn_gain,
    w_gate,
    w_up,
    w_down,
):
    shard_rows = tokens.shape[0]
    groups = H // KVH
    row_base = lax.axis_index("hid") * shard_rows
    positions = group_positions(segment, "hid")
    query_idx = row_base + jnp.arange(shard_rows, dtype=jnp.int32)
    seg_start = query_idx - positions
    resid = tokens.astype(jnp.float32)
    normed = rms_scale(resid, attn_gain).astype(jnp.bfloat16)
    q_raw = jnp.dot(normed, w_query, preferred_element_type=jnp.float32).reshape(shard_rows, H, HD)
    k_raw = jnp.dot(normed, w_key, preferred_element_type=jnp.float32).reshape(shard_rows, KVH, HD)
    queries = rotate(rms_scale(q_raw, q_gain), positions).astype(jnp.bfloat16)
    key_heads = (
        rotate(rms_scale(k_raw, k_gain), positions)
        .astype(jnp.bfloat16)
        .reshape(shard_rows, KVH * HD)
    )
    values = jnp.dot(normed, w_value, preferred_element_type=jnp.float32).astype(jnp.bfloat16)
    kv_cache = jnp.concatenate([key_heads, values], axis=1)
    q_grid = queries.reshape(shard_rows, KVH, groups, HD).transpose(1, 2, 0, 3)
    start_state = (
        jnp.full((KVH, groups, shard_rows), NEG_FILL, jnp.float32),
        jnp.zeros((KVH, groups, shard_rows), jnp.float32),
        jnp.zeros((KVH, groups, shard_rows, HD), jnp.float32),
    )
    hid_count = lax.psum(1, "hid")
    pieces = [kv_cache, w_gate, w_up, w_down]
    sizes = [p.size for p in pieces]
    bundle = lax.all_gather(
        jnp.concatenate([p.reshape(-1) for p in pieces]), "hid", axis=0, tiled=False
    )
    cuts = [sum(sizes[:i]) for i in range(len(sizes) + 1)]
    parts = [
        bundle[:, cuts[i] : cuts[i + 1]].reshape((hid_count * p.shape[0],) + p.shape[1:])
        for i, p in enumerate(pieces)
    ]
    kv_part, gate_rows, up_rows, down_rows = parts
    key_part = kv_part[:, : KVH * HD]
    val_part = kv_part[:, KVH * HD :]
    key_count = key_part.shape[0]
    blk_len = block_length(shard_rows)

    def one_block(block_idx, state_in):
        offset = jnp.asarray(block_idx, jnp.int32) * blk_len
        local_off = jnp.asarray(block_idx, jnp.int32) * blk_len
        key_blk = lax.dynamic_slice_in_dim(key_part, local_off, blk_len)
        val_blk = lax.dynamic_slice_in_dim(val_part, local_off, blk_len)
        key_idx = offset + jnp.arange(blk_len, dtype=jnp.int32)
        return key_block(state_in, key_blk, val_blk, key_idx, q_grid, seg_start, query_idx)

    run_peak, run_total, run_acc = lax.fori_loop(0, key_count // blk_len, one_block, start_state)
    attended = (
        (run_acc / run_total[..., None])
        .transpose(2, 0, 1, 3)
        .reshape(shard_rows, H * HD)
        .astype(jnp.bfloat16)
    )
    after_attn = (resid + jnp.dot(attended, w_out, preferred_element_type=jnp.float32)).astype(
        jnp.bfloat16
    )
    after_f32 = lax.optimization_barrier(after_attn).astype(jnp.float32)
    mlp_in = rms_scale(after_f32, ffn_gain).astype(jnp.bfloat16)
    gathered = lax.all_gather(mlp_in, "req", axis=0, tiled=True)
    unit_sum = unit_terms((gate_rows, up_rows, down_rows), gathered)
    own_share = lax.psum_scatter(
        unit_sum.astype(jnp.bfloat16), "req", scatter_dimension=0, tiled=True
    ).astype(jnp.float32)
    mixed = (after_f32 + own_share).astype(jnp.bfloat16)
    return (mixed, kv_cache)


def solution(mesh):
    placed = (
        P(("req", "hid"), None),
        P(("req", "hid")),
        P(),
        P(),
        P(),
        P(),
        P(),
        P(),
        P(),
        P(),
        P(("req", "hid"), None),
        P(("req", "hid"), None),
        P(("req", "hid"), None),
    )
    return jax.shard_map(
        per_device,
        mesh=mesh,
        in_specs=placed,
        out_specs=(P(("req", "hid"), None), P(("req", "hid"), None)),
        check_vma=False,
    )
```

profile of v0, /device:TPU:0, one launch (start us, length us, event | category | flops | bytes accessed | tf_op | source)
XLA Modules:
  0.0 388.1 jit_solution(17005629761590699012)
XLA Ops:
  7.2 1.4 fusion.34
  8.6 2.0 fusion.24
  11.9 1.3 pad_add_fusion
  13.3 3.9 %collective-permute-start = (s32[3]{0:T(128)S(1)}, s32[3]{0:T(128)S(1)}, u32[]{:S(2)}, u32[]{:S(2)}) collective-permute-start(s32[3]{0:T(128)S(1)} %pad_add_fusion), channel_id=1, source_target_pairs={{0,1},{1,2},{2,3},{3,4},{4,5},{5,6},{6,7},{7,8},{8,9},{9,10},{10,1... | collective-permute-start | bytes 44 | tf_op jit(solution)/shard_map/ppermute | solution.py:93
  17.2 0.8 slice_compare_fusion
  18.8 1.3 fusion.16
  20.0 1.1 reshape.220
  21.2 1.1 reshape.221
  22.2 1.1 reshape.222
  23.3 2.1 convolution_convert_fusion.1
  25.5 0.8 multiply_reduce_fusion.1
  30.2 1.3 broadcast_select_fusion
  31.6 0.7 fusion.41
  32.3 5.5 %collective-permute-start.1 = (s32[3]{0:T(128)S(1)}, s32[3]{0:T(128)S(1)}, u32[]{:S(2)}, u32[]{:S(2)}) collective-permute-start(s32[3]{0:T(128)S(1)} %broadcast_select_fusion), channel_id=1, source_target_pairs={{0,2},{1,3},{2,4},{3,5},{4,6},{5,7},{6,8},{7,9},{8,10},{9,11},{10,... | collective-permute-start | bytes 44 | tf_op jit(solution)/shard_map/ppermute | solution.py:93
  38.3 0.7 collective-permute-done.1
  43.0 2.0 broadcast_select_fusion.1
  45.6 4.4 %collective-permute-start.2 = (s32[3]{0:T(128)S(1)}, s32[3]{0:T(128)S(1)}, u32[]{:S(2)}, u32[]{:S(2)}) collective-permute-start(s32[3]{0:T(128)S(1)} %broadcast_select_fusion.1), channel_id=1, source_target_pairs={{0,4},{1,5},{2,6},{3,7},{4,8},{5,9},{6,10},{7,11},{8,12},{9,13},{1... | collective-permute-start | bytes 44 | tf_op jit(solution)/shard_map/ppermute | solution.py:93
  55.3 2.7 broadcast_select_fusion.2
  58.6 5.7 %collective-permute-start.3 = (s32[3]{0:T(128)S(1)}, s32[3]{0:T(128)S(1)}, u32[]{:S(2)}, u32[]{:S(2)}) collective-permute-start(s32[3]{0:T(128)S(1)} %broadcast_select_fusion.2), channel_id=1, source_target_pairs={{0,8},{1,9},{2,10},{3,11},{4,12},{5,13},{6,14},{7,15},{16,24},{17,... | collective-permute-start | bytes 44 | tf_op jit(solution)/shard_map/ppermute | solution.py:93
  69.4 3.2 broadcast_select_fusion.3
  72.6 3.8 collective-permute-start.4
  76.5 1.3 collective-permute-done.4
  80.8 0.9 pad_maximum_fusion
  81.9 4.3 %fusion.27 = f32[192,1536]{0,1:T(8,128)S(1)} fusion(bf16[1536,1536]{1,0:T(8,128)(2,1)} %param.18, bf16[192,1536]{1,0:T(8,128)(2,1)S(1)} %copy-done.12, f32[1536]{0:T(1024)S(1)} %copy-done.17, f32[192]{0:T(256)S(1)} %add_rsqrt_fusion.3), kind=kOutput, calls=%fused_computation.76 | convolution fusion | flops 907149312 | bytes 6494976 | tf_op jit(solution)/shard_map/dot_general | solution.py:129
  87.2 82.5 %all-gather.6.cloned.1.call-done = bf16[5799936]{0:T(1024)(128)(2,1)} async-done(((bf16[362496]{0:T(1024)(128)(2,1)}), bf16[5799936]{0:T(1024)(128)(2,1)}) %all-gather.6.cloned.1.call-update) | async-done | bytes 11599888 | tf_op jit(solution)/shard_map/all_gather | solution.py:148
  169.7 15.1 %reshape.228 = bf16[16,362496]{1,0:T(8,128)(2,1)} reshape(bf16[5799936]{0:T(1024)(128)(2,1)} %all-gather.6.cloned.1.call-done) | data formatting | bytes 23199744 | tf_op jit(solution)/shard_map/all_gather | solution.py:148
  184.8 6.4 %slice.164 = bf16[16,196608]{1,0:T(8,128)(2,1)} slice(bf16[16,362496]{1,0:T(8,128)(2,1)} %reshape.228), slice={[0:16], [0:196608]} | slice | bytes 12582912 | tf_op jit(solution)/shard_map/slice | solution.py:153
  191.2 6.4 %reshape.223 = bf16[3072,1024]{1,0:T(8,128)(2,1)} reshape(bf16[16,196608]{1,0:T(8,128)(2,1)} %slice.164) | data formatting | bytes 12582912 | tf_op jit(solution)/shard_map/reshape | solution.py:153
  197.6 5.9 %fusion.33 = (bf16[3072,512]{1,0:T(8,128)(2,1)}, bf16[3072,512]{1,0:T(8,128)(2,1)}) fusion(bf16[3072,1024]{1,0:T(8,128)(2,1)} %reshape.223), kind=kLoop, calls=%fused_computation.79 | loop fusion | bytes 12582912 | tf_op jit(solution)/shard_map/slice | solution.py:158
  203.6 75.3 %while.18 = (s32[]{:T(128)}, f32[8,3,192]{2,1,0:T(4,128)S(1)}, f32[8,3,192]{2,1,0:T(4,128)}, f32[8,3,192,64]{2,3,1,0:T(8,128)}, s32[192]{0:T(256)S(1)}, /*index=...) while((s32[]{:T(128)}, f32[8,3,192]{2,1,0:T(4,128)S(1)}, ...), condition=%wide.region_9.10_spmd.clone, body=%wide.region_6.9_spmd.clone.sunk | while | flops 953327040 | bytes 120382040 | solution.py:170
  203.8 1.5 constant_dynamic-slice_fusion.3
  205.8 3.0 fusion.70
  208.8 4.7 %fusion.71 = f32[8,3,192]{2,1,0:T(4,128)S(1)} fusion(f32[8,768,3,192]{1,3,2,0:T(8,128)S(1)} %get-tuple-element.337, f32[8,3,192]{2,1,0:T(4,128)S(1)} %select_maximum_fusion.2, pred[192,768]{1,0:T(8,128)(4,1)S(1)} %compare_and_fusion.2), kind=kLoop, calls=%fused_computation.5.clone.1 | loop fusion | flops 17690112 | bytes 14340096 | tf_op jit(solution)/shard_map/while/body/eval_jaxpr/reduce_sum | solution.py:57
  214.1 7.1 %fusion.73 = f32[8,3,192,64]{2,3,1,0:T(8,128)S(1)} fusion(f32[8,3,192,64]{2,3,1,0:T(8,128)S(1)} %copy-done.6, bf16[8,768,64,1]{1,2,3,0:T(8,128)(2,1)S(1)} %bitcast.87, f32[8,768,3,192]{1,3,2,0:T(8,128)} %copy-done.2, f32[8,3,192]{2,1,0:T(4,128)S(1)} %select_maximum_fusion.2, pred[192,768]{1,0:T(8,128)(4,1)S(1)} %compare_and_fusion.2, ...), kind=kOutput, calls=%fused_computation.9.clone.1 | convolution fusion | flops 471564288 | bytes 17485824 | tf_op jit(solution)/shard_map/while/body/eval_jaxpr/kgqc,kcd->kgqd/dot_general | solution.py:58
  221.3 1.1 copy-done.7
  222.6 1.5 constant_dynamic-slice_fusion.3
  224.6 3.0 fusion.70
  227.7 4.7 %fusion.71 = f32[8,3,192]{2,1,0:T(4,128)S(1)} fusion(f32[8,768,3,192]{1,3,2,0:T(8,128)S(1)} %get-tuple-element.337, f32[8,3,192]{2,1,0:T(4,128)S(1)} %select_maximum_fusion.2, pred[192,768]{1,0:T(8,128)(4,1)S(1)} %compare_and_fusion.2), kind=kLoop, calls=%fused_computation.5.clone.1 | loop fusion | flops 17690112 | bytes 14340096 | tf_op jit(solution)/shard_map/while/body/eval_jaxpr/reduce_sum | solution.py:57
  233.0 7.1 %fusion.73 = f32[8,3,192,64]{2,3,1,0:T(8,128)S(1)} fusion(f32[8,3,192,64]{2,3,1,0:T(8,128)S(1)} %copy-done.6, bf16[8,768,64,1]{1,2,3,0:T(8,128)(2,1)S(1)} %bitcast.87, f32[8,768,3,192]{1,3,2,0:T(8,128)} %copy-done.2, f32[8,3,192]{2,1,0:T(4,128)S(1)} %select_maximum_fusion.2, pred[192,768]{1,0:T(8,128)(4,1)S(1)} %compare_and_fusion.2, ...), kind=kOutput, calls=%fused_computation.9.clone.1 | convolution fusion | flops 471564288 | bytes 17485824 | tf_op jit(solution)/shard_map/while/body/eval_jaxpr/kgqc,kcd->kgqd/dot_general | solution.py:58
  240.1 1.1 copy-done.7
  241.4 1.5 constant_dynamic-slice_fusion.3
  243.5 3.0 fusion.70
  246.5 4.7 %fusion.71 = f32[8,3,192]{2,1,0:T(4,128)S(1)} fusion(f32[8,768,3,192]{1,3,2,0:T(8,128)S(1)} %get-tuple-element.337, f32[8,3,192]{2,1,0:T(4,128)S(1)} %select_maximum_fusion.2, pred[192,768]{1,0:T(8,128)(4,1)S(1)} %compare_and_fusion.2), kind=kLoop, calls=%fused_computation.5.clone.1 | loop fusion | flops 17690112 | bytes 14340096 | tf_op jit(solution)/shard_map/while/body/eval_jaxpr/reduce_sum | solution.py:57
  251.8 7.1 %fusion.73 = f32[8,3,192,64]{2,3,1,0:T(8,128)S(1)} fusion(f32[8,3,192,64]{2,3,1,0:T(8,128)S(1)} %copy-done.6, bf16[8,768,64,1]{1,2,3,0:T(8,128)(2,1)S(1)} %bitcast.87, f32[8,768,3,192]{1,3,2,0:T(8,128)} %copy-done.2, f32[8,3,192]{2,1,0:T(4,128)S(1)} %select_maximum_fusion.2, pred[192,768]{1,0:T(8,128)(4,1)S(1)} %compare_and_fusion.2, ...), kind=kOutput, calls=%fused_computation.9.clone.1 | convolution fusion | flops 471564288 | bytes 17485824 | tf_op jit(solution)/shard_map/while/body/eval_jaxpr/kgqc,kcd->kgqd/dot_general | solution.py:58
  258.9 1.1 copy-done.7
  260.3 1.5 constant_dynamic-slice_fusion.3
  262.3 3.0 fusion.70
  265.3 4.7 %fusion.71 = f32[8,3,192]{2,1,0:T(4,128)S(1)} fusion(f32[8,768,3,192]{1,3,2,0:T(8,128)S(1)} %get-tuple-element.337, f32[8,3,192]{2,1,0:T(4,128)S(1)} %select_maximum_fusion.2, pred[192,768]{1,0:T(8,128)(4,1)S(1)} %compare_and_fusion.2), kind=kLoop, calls=%fused_computation.5.clone.1 | loop fusion | flops 17690112 | bytes 14340096 | tf_op jit(solution)/shard_map/while/body/eval_jaxpr/reduce_sum | solution.py:57
  270.6 7.1 %fusion.73 = f32[8,3,192,64]{2,3,1,0:T(8,128)S(1)} fusion(f32[8,3,192,64]{2,3,1,0:T(8,128)S(1)} %copy-done.6, bf16[8,768,64,1]{1,2,3,0:T(8,128)(2,1)S(1)} %bitcast.87, f32[8,768,3,192]{1,3,2,0:T(8,128)} %copy-done.2, f32[8,3,192]{2,1,0:T(4,128)S(1)} %select_maximum_fusion.2, pred[192,768]{1,0:T(8,128)(4,1)S(1)} %compare_and_fusion.2, ...), kind=kOutput, calls=%fused_computation.9.clone.1 | convolution fusion | flops 471564288 | bytes 17485824 | tf_op jit(solution)/shard_map/while/body/eval_jaxpr/kgqc,kcd->kgqd/dot_general | solution.py:58
  277.7 1.1 copy-done.7
  278.9 1.7 divide_convert_fusion
  280.6 3.4 fusion.15
  284.2 1.1 fusion.21
  285.4 4.7 %fusion.32 = (bf16[16,55296]{1,0:T(8,128)(2,1)}, bf16[16,55296]{1,0:T(8,128)(2,1)}, bf16[16,55296]{1,0:T(8,128)(2,1)S(1)}) fusion(bf16[16,362496]{1,0:T(8,128)(2,1)} %reshape.228), kind=kLoop, calls=%fused_computation.78 | loop fusion | bytes 10616832 | tf_op jit(solution)/shard_map/slice | solution.py:153
  290.0 4.8 %reshape.226 = bf16[576,1536]{1,0:T(8,128)(2,1)} reshape(bf16[16,55296]{1,0:T(8,128)(2,1)} %get-tuple-element.234) | data formatting | bytes 3538944 | tf_op jit(solution)/shard_map/reshape | solution.py:153
  294.8 4.8 %reshape.227 = bf16[576,1536]{1,0:T(8,128)(2,1)} reshape(bf16[16,55296]{1,0:T(8,128)(2,1)} %get-tuple-element.235) | data formatting | bytes 3538944 | tf_op jit(solution)/shard_map/reshape | solution.py:153
  299.7 3.7 reshape.225
  303.3 16.0 %all-gather.4.cloned.1.call-done = bf16[1536,1536]{1,0:T(8,128)(2,1)} async-done(((bf16[192,1536]{1,0:T(8,128)(2,1)}), bf16[1536,1536]{1,0:T(8,128)(2,1)}) %all-gather.4.cloned.1.call-update) | async-done | bytes 4718608 | tf_op jit(solution)/shard_map/all_gather | solution.py:182
  319.4 7.7 %fusion.43 = f32[1536,576]{0,1:T(8,128)} fusion(bf16[1536,1536]{1,0:T(8,128)(2,1)} %all-gather.4.cloned.1.call-done, bf16[576,1536]{1,0:T(8,128)(2,1)} %reshape.225), kind=kOutput, calls=%fused_computation.89 | convolution fusion | flops 2717908992 | bytes 10027008 | tf_op jit(solution)/shard_map/dot_general | solution.py:67
  327.0 13.3 %convolution_convert_fusion = bf16[1536,1536]{1,0:T(8,128)(2,1)} fusion(bf16[576,1536]{1,0:T(8,128)(2,1)} %reshape.227, f32[1536,576]{0,1:T(8,128)} %fusion.43, bf16[1536,1536]{1,0:T(8,128)(2,1)} %all-gather.4.cloned.1.call-done, bf16[576,1536]{1,0:T(8,128)(2,1)S(1)} %copy-done.5), kind=kOutput, calls=%fused_computation.22 | convolution fusion | flops 5443485696 | bytes 16515072 | tf_op jit(solution)/shard_map/dot_general | solution.py:70
  340.4 0.9 copy-done.11
  341.3 0.8 pad_maximum_fusion.1
  342.1 37.5 %reduce-scatter.2.cloned.1.call-done = bf16[192,1536]{1,0:T(8,128)(2,1)} async-done(((bf16[1536,1536]{1,0:T(8,128)(2,1)}), bf16[192,1536]{1,0:T(8,128)(2,1)}) %reduce-scatter.2.cloned.1.call-update) | async-done | bytes 589840 | tf_op jit(solution)/shard_map/reduce_scatter | solution.py:184
  379.6 2.0 fusion.22
  (137 shorter events, 14.0 us)
Async XLA Ops:
  7.2 18.3 %copy-start = (bf16[1536,512]{1,0:T(8,128)(2,1)S(1)}, bf16[1536,512]{1,0:T(8,128)(2,1)}, u32[]{:S(2)}) copy-start(bf16[1536,512]{1,0:T(8,128)(2,1)} %param.19) | copy-start | bytes 4718596
  7.2 162.5 %all-gather.6.cloned.1.call-start = ((), (), s32[]{:S(2)}) async-start(), calls=%async_computation.3 | async-start | bytes 12324864 | tf_op jit(solution)/shard_map/all_gather | solution.py:148
  13.3 13.1 %collective-permute-start = (s32[3]{0:T(128)S(1)}, s32[3]{0:T(128)S(1)}, u32[]{:S(2)}, u32[]{:S(2)}) collective-permute-start(s32[3]{0:T(128)S(1)} %pad_add_fusion), channel_id=1, source_target_pairs={{0,1},{1,2},{2,3},{3,4},{4,5},{5,6},{6,7},{7,8},{8,9},{9,10},{10,1... | collective-permute-start | bytes 44 | tf_op jit(solution)/shard_map/ppermute | solution.py:93
  20.0 5.4 %copy-start.12 = (bf16[192,1536]{1,0:T(8,128)(2,1)S(1)}, bf16[192,1536]{1,0:T(8,128)(2,1)}, u32[]{:S(2)}) copy-start(bf16[192,1536]{1,0:T(8,128)(2,1)} %param.15) | copy-start | bytes 1769476
  20.0 5.4 %copy-start.17 = (f32[1536]{0:T(1024)S(1)}, f32[1536]{0:T(1024)}, u32[]{:S(2)}) copy-start(f32[1536]{0:T(1024)} %param.17) | copy-start | bytes 18436
  25.5 55.2 %copy-start.10 = (bf16[192,512]{1,0:T(8,128)(2,1)}, bf16[192,512]{1,0:T(8,128)(2,1)S(1)}, u32[]{:S(2)}) copy-start(bf16[192,512]{1,0:T(8,128)(2,1)S(1)} %convolution_convert_fusion.1) | copy-start | bytes 589828
  25.5 0.8 copy-start.15
  32.3 6.8 %collective-permute-start.1 = (s32[3]{0:T(128)S(1)}, s32[3]{0:T(128)S(1)}, u32[]{:S(2)}, u32[]{:S(2)}) collective-permute-start(s32[3]{0:T(128)S(1)} %broadcast_select_fusion), channel_id=1, source_target_pairs={{0,2},{1,3},{2,4},{3,5},{4,6},{5,7},{6,8},{7,9},{8,10},{9,11},{10,... | collective-permute-start | bytes 44 | tf_op jit(solution)/shard_map/ppermute | solution.py:93
  45.6 5.7 %collective-permute-start.2 = (s32[3]{0:T(128)S(1)}, s32[3]{0:T(128)S(1)}, u32[]{:S(2)}, u32[]{:S(2)}) collective-permute-start(s32[3]{0:T(128)S(1)} %broadcast_select_fusion.1), channel_id=1, source_target_pairs={{0,4},{1,5},{2,6},{3,7},{4,8},{5,9},{6,10},{7,11},{8,12},{9,13},{1... | collective-permute-start | bytes 44 | tf_op jit(solution)/shard_map/ppermute | solution.py:93
  58.6 7.0 %collective-permute-start.3 = (s32[3]{0:T(128)S(1)}, s32[3]{0:T(128)S(1)}, u32[]{:S(2)}, u32[]{:S(2)}) collective-permute-start(s32[3]{0:T(128)S(1)} %broadcast_select_fusion.2), channel_id=1, source_target_pairs={{0,8},{1,9},{2,10},{3,11},{4,12},{5,13},{6,14},{7,15},{16,24},{17,... | collective-permute-start | bytes 44 | tf_op jit(solution)/shard_map/ppermute | solution.py:93
  72.6 5.1 %collective-permute-start.4 = (s32[3]{0:T(128)S(1)}, s32[3]{0:T(128)S(1)}, u32[]{:S(2)}, u32[]{:S(2)}) collective-permute-start(s32[3]{0:T(128)S(1)} %broadcast_select_fusion.3), channel_id=1, source_target_pairs={{0,1},{1,2},{2,3},{3,4},{4,5},{5,6},{6,7},{7,8},{8,9},{9,10},{10,1... | collective-permute-start | bytes 44 | tf_op jit(solution)/shard_map/ppermute | solution.py:99
  81.8 237.6 %all-gather.4.cloned.1.call-start = ((), (), s32[]{:S(2)}) async-start(), calls=%async_computation.1 | async-start | bytes 5308416 | tf_op jit(solution)/shard_map/all_gather | solution.py:182
  81.8 4.6 %copy-start.16 = (f32[64]{0:T(128)S(1)}, f32[64]{0:T(128)}, u32[]{:S(2)}) copy-start(f32[64]{0:T(128)} %param.21) | copy-start | bytes 772
  208.8 5.3 %copy-start.2 = (f32[8,768,3,192]{1,3,2,0:T(8,128)}, f32[8,768,3,192]{1,3,2,0:T(8,128)S(1)}, u32[]{:S(2)}) copy-start(f32[8,768,3,192]{1,3,2,0:T(8,128)S(1)} %get-tuple-element.337) | copy-start | bytes 42467332 | tf_op jit(solution)/shard_map/while
  208.8 5.3 %copy-start.8 = (f32[8,3,192]{2,1,0:T(4,128)S(1)}, f32[8,3,192]{2,1,0:T(4,128)}, u32[]{:S(2)}) copy-start(f32[8,3,192]{2,1,0:T(4,128)} %get-tuple-element.356) | copy-start | bytes 55300 | tf_op jit(solution)/shard_map/while
  208.8 5.3 %copy-start.6 = (f32[8,3,192,64]{2,3,1,0:T(8,128)S(1)}, f32[8,3,192,64]{2,3,1,0:T(8,128)}, u32[]{:S(2)}) copy-start(f32[8,3,192,64]{2,3,1,0:T(8,128)} %get-tuple-element.357) | copy-start | bytes 3538948 | tf_op jit(solution)/shard_map/while
  214.1 7.1 %copy-start.9 = (f32[8,3,192]{2,1,0:T(4,128)}, f32[8,3,192]{2,1,0:T(4,128)S(1)}, u32[]{:S(2)}) copy-start(f32[8,3,192]{2,1,0:T(4,128)S(1)} %get-tuple-element.369) | copy-start | bytes 55300 | tf_op jit(solution)/shard_map/while
  221.2 1.2 copy-start.7
  227.6 5.3 %copy-start.2 = (f32[8,768,3,192]{1,3,2,0:T(8,128)}, f32[8,768,3,192]{1,3,2,0:T(8,128)S(1)}, u32[]{:S(2)}) copy-start(f32[8,768,3,192]{1,3,2,0:T(8,128)S(1)} %get-tuple-element.337) | copy-start | bytes 42467332 | tf_op jit(solution)/shard_map/while
  227.6 5.3 %copy-start.8 = (f32[8,3,192]{2,1,0:T(4,128)S(1)}, f32[8,3,192]{2,1,0:T(4,128)}, u32[]{:S(2)}) copy-start(f32[8,3,192]{2,1,0:T(4,128)} %get-tuple-element.356) | copy-start | bytes 55300 | tf_op jit(solution)/shard_map/while
  227.6 5.3 %copy-start.6 = (f32[8,3,192,64]{2,3,1,0:T(8,128)S(1)}, f32[8,3,192,64]{2,3,1,0:T(8,128)}, u32[]{:S(2)}) copy-start(f32[8,3,192,64]{2,3,1,0:T(8,128)} %get-tuple-element.357) | copy-start | bytes 3538948 | tf_op jit(solution)/shard_map/while
  232.9 7.1 %copy-start.9 = (f32[8,3,192]{2,1,0:T(4,128)}, f32[8,3,192]{2,1,0:T(4,128)S(1)}, u32[]{:S(2)}) copy-start(f32[8,3,192]{2,1,0:T(4,128)S(1)} %get-tuple-element.369) | copy-start | bytes 55300 | tf_op jit(solution)/shard_map/while
  240.1 1.2 copy-start.7
  246.4 5.3 %copy-start.2 = (f32[8,768,3,192]{1,3,2,0:T(8,128)}, f32[8,768,3,192]{1,3,2,0:T(8,128)S(1)}, u32[]{:S(2)}) copy-start(f32[8,768,3,192]{1,3,2,0:T(8,128)S(1)} %get-tuple-element.337) | copy-start | bytes 42467332 | tf_op jit(solution)/shard_map/while
  246.5 5.3 %copy-start.8 = (f32[8,3,192]{2,1,0:T(4,128)S(1)}, f32[8,3,192]{2,1,0:T(4,128)}, u32[]{:S(2)}) copy-start(f32[8,3,192]{2,1,0:T(4,128)} %get-tuple-element.356) | copy-start | bytes 55300 | tf_op jit(solution)/shard_map/while
  246.5 5.3 %copy-start.6 = (f32[8,3,192,64]{2,3,1,0:T(8,128)S(1)}, f32[8,3,192,64]{2,3,1,0:T(8,128)}, u32[]{:S(2)}) copy-start(f32[8,3,192,64]{2,3,1,0:T(8,128)} %get-tuple-element.357) | copy-start | bytes 3538948 | tf_op jit(solution)/shard_map/while
  251.8 7.1 %copy-start.9 = (f32[8,3,192]{2,1,0:T(4,128)}, f32[8,3,192]{2,1,0:T(4,128)S(1)}, u32[]{:S(2)}) copy-start(f32[8,3,192]{2,1,0:T(4,128)S(1)} %get-tuple-element.369) | copy-start | bytes 55300 | tf_op jit(solution)/shard_map/while
  258.9 1.2 copy-start.7
  265.3 5.3 %copy-start.2 = (f32[8,768,3,192]{1,3,2,0:T(8,128)}, f32[8,768,3,192]{1,3,2,0:T(8,128)S(1)}, u32[]{:S(2)}) copy-start(f32[8,768,3,192]{1,3,2,0:T(8,128)S(1)} %get-tuple-element.337) | copy-start | bytes 42467332 | tf_op jit(solution)/shard_map/while
  265.3 5.3 %copy-start.8 = (f32[8,3,192]{2,1,0:T(4,128)S(1)}, f32[8,3,192]{2,1,0:T(4,128)}, u32[]{:S(2)}) copy-start(f32[8,3,192]{2,1,0:T(4,128)} %get-tuple-element.356) | copy-start | bytes 55300 | tf_op jit(solution)/shard_map/while
  265.3 5.3 %copy-start.6 = (f32[8,3,192,64]{2,3,1,0:T(8,128)S(1)}, f32[8,3,192,64]{2,3,1,0:T(8,128)}, u32[]{:S(2)}) copy-start(f32[8,3,192,64]{2,3,1,0:T(8,128)} %get-tuple-element.357) | copy-start | bytes 3538948 | tf_op jit(solution)/shard_map/while
  270.6 7.1 %copy-start.9 = (f32[8,3,192]{2,1,0:T(4,128)}, f32[8,3,192]{2,1,0:T(4,128)S(1)}, u32[]{:S(2)}) copy-start(f32[8,3,192]{2,1,0:T(4,128)S(1)} %get-tuple-element.369) | copy-start | bytes 55300 | tf_op jit(solution)/shard_map/while
  277.7 1.2 copy-start.7
  278.9 1.7 copy-start.13
  280.5 3.7 copy-start.14
  284.0 6.0 %copy-start.3 = (bf16[192,1536]{1,0:T(8,128)(2,1)}, bf16[192,1536]{1,0:T(8,128)(2,1)S(1)}, u32[]{:S(2)}) copy-start(bf16[192,1536]{1,0:T(8,128)(2,1)S(1)} %fusion.15) | copy-start | bytes 1769476
  285.3 94.3 %reduce-scatter.2.cloned.1.call-start = ((), (), s32[]{:S(2)}) async-start(), calls=%async_computation.2 | async-start | bytes 5308416 | tf_op jit(solution)/shard_map/reduce_scatter | solution.py:184
  303.3 23.7 %copy-start.5 = (bf16[576,1536]{1,0:T(8,128)(2,1)S(1)}, bf16[576,1536]{1,0:T(8,128)(2,1)}, u32[]{:S(2)}) copy-start(bf16[576,1536]{1,0:T(8,128)(2,1)} %reshape.226) | copy-start | bytes 5308420
  340.4 0.9 copy-start.11
  340.4 39.2 %copy-start.4 = (bf16[192,1536]{1,0:T(8,128)(2,1)S(1)}, bf16[192,1536]{1,0:T(8,128)(2,1)}, u32[]{:S(2)}) copy-start(bf16[192,1536]{1,0:T(8,128)(2,1)} %copy-done.3) | copy-start | bytes 1769476
  341.3 40.3 %copy-start.1 = (bf16[1536,512]{1,0:T(8,128)(2,1)S(1)}, bf16[1536,512]{1,0:T(8,128)(2,1)}, u32[]{:S(2)}) copy-start(bf16[1536,512]{1,0:T(8,128)(2,1)} %param.19) | copy-start | bytes 4718596
Sparse Core Ops, SparseCore 0:
  81.9 87.7 all-gather.5
  285.4 33.8 all-gather.3
  340.5 38.9 reduce-scatter.1
where the time goes:
time: 389 us; the launch traced here: 388 us
  waiting for transfers between devices  139 us (36%)
  local copies, waits for them, and re-layouts  78 us (20%)
  matrix products  71.9 us (18%)
  other arithmetic  42.9 us (11%)
  between operations  32.2 us (8%)
  starting transfers between devices  23.4 us (6%)
    all_gather x1, waiting for transfers between devices, per_device(): lax.all_gather(jnp.concatenate([p.reshape(-1) for p in pieces]), 'hid', a...  82.5 us
    reduce_scatter x1, waiting for transfers between devices, per_device(): lax.psum_scatter(unit_sum.astype(jnp.bfloat16), 'req', scatter_dimension=...  37.5 us
    dot_general x4, matrix products, key_block(): jnp.einsum('kgqc,kcd->kgqd', weights.astype(jnp.bfloat16), v_grid, prefer...  28.4 us
    reshape x4, local copies, waits for them, and re-layouts, per_device(): bundle[:, cuts[i]:cuts[i + 1]]  19.7 us
    ppermute x4, starting transfers between devices, group_positions(): got = lax.ppermute(summary, axis, pairs)  19.5 us
    reduce_sum x4, other arithmetic, key_block(): new_total = run_total * factor + jnp.sum(weights, axis=-1)  18.8 us
    all_gather x1, waiting for transfers between devices, per_device(): gathered = lax.all_gather(mlp_in, 'req', axis=0, tiled=True)  16 us
    all_gather x1, local copies, waits for them, and re-layouts, per_device(): lax.all_gather(jnp.concatenate([p.reshape(-1) for p in pieces]), 'hid', a...  15.1 us
  transfers between devices with their start and end apart: 8, of which 7 were waited for; matrix products, arithmetic and copies ran while one was open for 9% of the time, Pallas kernels for 0%

commit v1 on v0

--- a/solution.py
+++ b/solution.py
@@ -10,6 +10,16 @@
 ROPE_BASE = 1000000.0
 NEG_FILL = -1e30
 SCORE_SCALE = 0.125
+
+
+def turned_line(value, mesh_axis, along):
+    size = lax.axis_size(mesh_axis)
+    current, tiles = (value, [value])
+    for _ in range(size - 1):
+        current = lax.ppermute(current, mesh_axis, [(i, (i + 1) % size) for i in range(size)])
+        tiles.insert(0, current)
+    line = jnp.concatenate(tiles, axis=along)
+    return jnp.roll(line, (lax.axis_index(mesh_axis) + 1) * value.shape[along], axis=along)
 
 
 def rms_scale(values, gain):
@@ -179,7 +189,7 @@
     )
     after_f32 = lax.optimization_barrier(after_attn).astype(jnp.float32)
     mlp_in = rms_scale(after_f32, ffn_gain).astype(jnp.bfloat16)
-    gathered = lax.all_gather(mlp_in, "req", axis=0, tiled=True)
+    gathered = turned_line(mlp_in, "req", 0)
     unit_sum = unit_terms((gate_rows, up_rows, down_rows), gathered)
     own_share = lax.psum_scatter(
         unit_sum.astype(jnp.bfloat16), "req", scatter_dimension=0, tiled=True

time: 389 us -> 446 us (1.15)
  waiting for transfers between devices: 139 us -> 186 us
  local copies, waits for them, and re-layouts: 78 us -> 90.1 us
    ppermute x0 -> x7, waiting for transfers between devices: none -> 63.5 us  [turned_line(): lax.ppermute(current, mesh_axis, [(i, (i + 1) % size) for i in range(size)])]
    all_gather x1 -> x0, waiting for transfers between devices: 16 us -> none  [per_device(): gathered = lax.all_gather(mlp_in, 'req', axis=0, tiled=True)]
    unnamed x27 -> x41, local copies, waits for them, and re-layouts: 1.04 us -> 11.9 us
  transfers between devices with their start and end apart: 8 -> 14, of which waited for: 7 -> 12; matrix products, arithmetic and copies ran while one was open for 9% -> 8% of each run, Pallas kernels for 0% -> 0%
where the time goes in v1:
time: 446 us; the launch traced here: 445 us
  waiting for transfers between devices  186 us (42%)
  local copies, waits for them, and re-layouts  90.1 us (20%)
  matrix products  69.7 us (16%)
  other arithmetic  42.4 us (10%)
  between operations  32.5 us (7%)
  starting transfers between devices  23.4 us (5%)
    all_gather x1, waiting for transfers between devices, per_device(): lax.all_gather(jnp.concatenate([p.reshape(-1) for p in pieces]), 'hid', a...  82.5 us
    ppermute x7, waiting for transfers between devices, turned_line(): lax.ppermute(current, mesh_axis, [(i, (i + 1) % size) for i in range(size)])  63.5 us
    reduce_scatter x1, waiting for transfers between devices, per_device(): lax.psum_scatter(unit_sum.astype(jnp.bfloat16), 'req', scatter_dimension=...  37 us
    dot_general x4, matrix products, key_block(): jnp.einsum('kgqc,kcd->kgqd', weights.astype(jnp.bfloat16), v_grid, prefer...  28.4 us
    reshape x4, local copies, waits for them, and re-layouts, per_device(): bundle[:, cuts[i]:cuts[i + 1]]  20.8 us
    ppermute x4, starting transfers between devices, group_positions(): got = lax.ppermute(summary, axis, pairs)  19.5 us
    reduce_sum x4, other arithmetic, key_block(): new_total = run_total * factor + jnp.sum(weights, axis=-1)  18.8 us
    all_gather x1, local copies, waits for them, and re-layouts, per_device(): lax.all_gather(jnp.concatenate([p.reshape(-1) for p in pieces]), 'hid', a...  15.1 us
  transfers between devices with their start and end apart: 14, of which 12 were waited for; matrix products, arithmetic and copies ran while one was open for 8% of the time, Pallas kernels for 0%

profile of v1, /device:TPU:0, one launch (start us, length us, event | category | flops | bytes accessed | tf_op | source)
XLA Modules:
  0.0 444.7 jit_solution(11956148769234451914)
XLA Ops:
  7.2 1.4 fusion.46
  8.7 2.0 fusion.33
  12.0 1.3 pad_add_fusion
  13.3 3.9 collective-permute-start
  18.8 1.3 fusion.25
  23.3 2.1 convolution_convert_fusion.1
  30.2 1.3 broadcast_select_fusion
  32.2 5.5 %collective-permute-start.1 = (s32[3]{0:T(128)S(1)}, s32[3]{0:T(128)S(1)}, u32[]{:S(2)}, u32[]{:S(2)}) collective-permute-start(s32[3]{0:T(128)S(1)} %broadcast_select_fusion), channel_id=1, source_target_pairs={{0,2},{1,3},{2,4},{3,5},{4,6},{5,7},{6,8},{7,9},{8,10},{9,11},{10,... | collective-permute-start | bytes 44 | tf_op jit(solution)/shard_map/ppermute | solution.py:103
  42.9 1.9 broadcast_select_fusion.1
  45.4 4.4 %collective-permute-start.2 = (s32[3]{0:T(128)S(1)}, s32[3]{0:T(128)S(1)}, u32[]{:S(2)}, u32[]{:S(2)}) collective-permute-start(s32[3]{0:T(128)S(1)} %broadcast_select_fusion.1), channel_id=1, source_target_pairs={{0,4},{1,5},{2,6},{3,7},{4,8},{5,9},{6,10},{7,11},{8,12},{9,13},{1... | collective-permute-start | bytes 44 | tf_op jit(solution)/shard_map/ppermute | solution.py:103
  55.2 2.6 broadcast_select_fusion.2
  58.4 5.7 %collective-permute-start.3 = (s32[3]{0:T(128)S(1)}, s32[3]{0:T(128)S(1)}, u32[]{:S(2)}, u32[]{:S(2)}) collective-permute-start(s32[3]{0:T(128)S(1)} %broadcast_select_fusion.2), channel_id=1, source_target_pairs={{0,8},{1,9},{2,10},{3,11},{4,12},{5,13},{6,14},{7,15},{16,24},{17,... | collective-permute-start | bytes 44 | tf_op jit(solution)/shard_map/ppermute | solution.py:103
  69.2 3.3 broadcast_select_fusion.3
  72.5 3.8 collective-permute-start.4
  76.3 1.3 collective-permute-done.4
  81.8 4.3 fusion.39
  87.1 82.5 %all-gather.3.cloned.1.call-done = bf16[5799936]{0:T(1024)(128)(2,1)} async-done(((bf16[362496]{0:T(1024)(128)(2,1)}), bf16[5799936]{0:T(1024)(128)(2,1)}) %all-gather.3.cloned.1.call-update) | async-done | bytes 11599888 | tf_op jit(solution)/shard_map/all_gather | solution.py:158
  169.6 15.1 %reshape.228 = bf16[16,362496]{1,0:T(8,128)(2,1)} reshape(bf16[5799936]{0:T(1024)(128)(2,1)} %all-gather.3.cloned.1.call-done) | data formatting | bytes 23199744 | tf_op jit(solution)/shard_map/all_gather | solution.py:158
  184.6 6.4 %slice.164 = bf16[16,196608]{1,0:T(8,128)(2,1)} slice(bf16[16,362496]{1,0:T(8,128)(2,1)} %reshape.228), slice={[0:16], [0:196608]} | slice | bytes 12582912 | tf_op jit(solution)/shard_map/slice | solution.py:163
  191.1 6.4 %reshape.223 = bf16[3072,1024]{1,0:T(8,128)(2,1)} reshape(bf16[16,196608]{1,0:T(8,128)(2,1)} %slice.164) | data formatting | bytes 12582912 | tf_op jit(solution)/shard_map/reshape | solution.py:163
  197.5 6.0 %fusion.45 = (bf16[3072,512]{1,0:T(8,128)(2,1)}, bf16[3072,512]{1,0:T(8,128)(2,1)}) fusion(bf16[3072,1024]{1,0:T(8,128)(2,1)} %reshape.223), kind=kLoop, calls=%fused_computation.102 | loop fusion | bytes 12582912 | tf_op jit(solution)/shard_map/slice | solution.py:168
  203.4 75.2 %while.18 = (s32[]{:T(128)}, f32[8,3,192]{2,1,0:T(4,128)S(1)}, f32[8,3,192]{2,1,0:T(4,128)S(1)}, f32[8,3,192,64]{2,3,1,0:T(8,128)}, s32[192]{0:T(256)S(1)}, /*in...) while((s32[]{:T(128)}, f32[8,3,192]{2,1,0:T(4,128)S(1)}, ...), condition=%wide.region_9.10_spmd.clone, body=%wide.region_6.9_spmd.clone.sunk | while | flops 953327040 | bytes 120234520 | solution.py:180
  203.6 1.5 constant_dynamic-slice_fusion.3
  205.7 3.0 fusion.79
  208.7 4.7 %fusion.80 = f32[8,3,192]{2,1,0:T(4,128)S(1)} fusion(f32[8,768,3,192]{1,3,2,0:T(8,128)S(1)} %get-tuple-element.337, f32[8,3,192]{2,1,0:T(4,128)S(1)} %select_maximum_fusion.2, pred[192,768]{1,0:T(8,128)(4,1)S(1)} %compare_and_fusion.2), kind=kLoop, calls=%fused_computation.5.clone.1 | loop fusion | flops 17690112 | bytes 14340096 | tf_op jit(solution)/shard_map/while/body/eval_jaxpr/reduce_sum | solution.py:67
  214.0 7.1 %fusion.82 = f32[8,3,192,64]{2,3,1,0:T(8,128)S(1)} fusion(f32[8,3,192,64]{2,3,1,0:T(8,128)S(1)} %copy-done.6, bf16[8,768,64,1]{1,2,3,0:T(8,128)(2,1)S(1)} %bitcast.85, f32[8,768,3,192]{1,3,2,0:T(8,128)} %copy-done.2, f32[8,3,192]{2,1,0:T(4,128)S(1)} %select_maximum_fusion.2, pred[192,768]{1,0:T(8,128)(4,1)S(1)} %compare_and_fusion.2, ...), kind=kOutput, calls=%fused_computation.9.clone.1 | convolution fusion | flops 471564288 | bytes 17485824 | tf_op jit(solution)/shard_map/while/body/eval_jaxpr/kgqc,kcd->kgqd/dot_general | solution.py:68
  221.1 1.1 copy-done.7
  222.4 1.5 constant_dynamic-slice_fusion.3
  224.5 3.0 fusion.79
  227.5 4.7 %fusion.80 = f32[8,3,192]{2,1,0:T(4,128)S(1)} fusion(f32[8,768,3,192]{1,3,2,0:T(8,128)S(1)} %get-tuple-element.337, f32[8,3,192]{2,1,0:T(4,128)S(1)} %select_maximum_fusion.2, pred[192,768]{1,0:T(8,128)(4,1)S(1)} %compare_and_fusion.2), kind=kLoop, calls=%fused_computation.5.clone.1 | loop fusion | flops 17690112 | bytes 14340096 | tf_op jit(solution)/shard_map/while/body/eval_jaxpr/reduce_sum | solution.py:67
  232.8 7.1 %fusion.82 = f32[8,3,192,64]{2,3,1,0:T(8,128)S(1)} fusion(f32[8,3,192,64]{2,3,1,0:T(8,128)S(1)} %copy-done.6, bf16[8,768,64,1]{1,2,3,0:T(8,128)(2,1)S(1)} %bitcast.85, f32[8,768,3,192]{1,3,2,0:T(8,128)} %copy-done.2, f32[8,3,192]{2,1,0:T(4,128)S(1)} %select_maximum_fusion.2, pred[192,768]{1,0:T(8,128)(4,1)S(1)} %compare_and_fusion.2, ...), kind=kOutput, calls=%fused_computation.9.clone.1 | convolution fusion | flops 471564288 | bytes 17485824 | tf_op jit(solution)/shard_map/while/body/eval_jaxpr/kgqc,kcd->kgqd/dot_general | solution.py:68
  239.9 1.1 copy-done.7
  241.2 1.5 constant_dynamic-slice_fusion.3
  243.3 3.0 fusion.79
  246.3 4.7 %fusion.80 = f32[8,3,192]{2,1,0:T(4,128)S(1)} fusion(f32[8,768,3,192]{1,3,2,0:T(8,128)S(1)} %get-tuple-element.337, f32[8,3,192]{2,1,0:T(4,128)S(1)} %select_maximum_fusion.2, pred[192,768]{1,0:T(8,128)(4,1)S(1)} %compare_and_fusion.2), kind=kLoop, calls=%fused_computation.5.clone.1 | loop fusion | flops 17690112 | bytes 14340096 | tf_op jit(solution)/shard_map/while/body/eval_jaxpr/reduce_sum | solution.py:67
  251.5 7.1 %fusion.82 = f32[8,3,192,64]{2,3,1,0:T(8,128)S(1)} fusion(f32[8,3,192,64]{2,3,1,0:T(8,128)S(1)} %copy-done.6, bf16[8,768,64,1]{1,2,3,0:T(8,128)(2,1)S(1)} %bitcast.85, f32[8,768,3,192]{1,3,2,0:T(8,128)} %copy-done.2, f32[8,3,192]{2,1,0:T(4,128)S(1)} %select_maximum_fusion.2, pred[192,768]{1,0:T(8,128)(4,1)S(1)} %compare_and_fusion.2, ...), kind=kOutput, calls=%fused_computation.9.clone.1 | convolution fusion | flops 471564288 | bytes 17485824 | tf_op jit(solution)/shard_map/while/body/eval_jaxpr/kgqc,kcd->kgqd/dot_general | solution.py:68
  258.7 1.1 copy-done.7
  260.0 1.5 constant_dynamic-slice_fusion.3
  262.0 3.0 fusion.79
  265.1 4.7 %fusion.80 = f32[8,3,192]{2,1,0:T(4,128)S(1)} fusion(f32[8,768,3,192]{1,3,2,0:T(8,128)S(1)} %get-tuple-element.337, f32[8,3,192]{2,1,0:T(4,128)S(1)} %select_maximum_fusion.2, pred[192,768]{1,0:T(8,128)(4,1)S(1)} %compare_and_fusion.2), kind=kLoop, calls=%fused_computation.5.clone.1 | loop fusion | flops 17690112 | bytes 14340096 | tf_op jit(solution)/shard_map/while/body/eval_jaxpr/reduce_sum | solution.py:67
  270.3 7.1 %fusion.82 = f32[8,3,192,64]{2,3,1,0:T(8,128)S(1)} fusion(f32[8,3,192,64]{2,3,1,0:T(8,128)S(1)} %copy-done.6, bf16[8,768,64,1]{1,2,3,0:T(8,128)(2,1)S(1)} %bitcast.85, f32[8,768,3,192]{1,3,2,0:T(8,128)} %copy-done.2, f32[8,3,192]{2,1,0:T(4,128)S(1)} %select_maximum_fusion.2, pred[192,768]{1,0:T(8,128)(4,1)S(1)} %compare_and_fusion.2, ...), kind=kOutput, calls=%fused_computation.9.clone.1 | convolution fusion | flops 471564288 | bytes 17485824 | tf_op jit(solution)/shard_map/while/body/eval_jaxpr/kgqc,kcd->kgqd/dot_general | solution.py:68
  277.5 1.1 copy-done.7
  278.6 1.6 divide_convert_fusion
  280.2 3.6 fusion.19
  284.3 10.5 %collective-permute-done.5 = bf16[192,1536]{1,0:T(8,128)(2,1)S(1)} collective-permute-done((bf16[192,1536]{1,0:T(8,128)(2,1)S(1)}, bf16[192,1536]{1,0:T(8,128)(2,1)S(1)}, u32[]{:S(2)}, u32[]{:S(2)}) %collective-permute-start.5) | collective-permute-done | bytes 589856 | tf_op jit(solution)/shard_map/ppermute | solution.py:19
  294.8 10.5 %collective-permute-done.6 = bf16[192,1536]{1,0:T(8,128)(2,1)S(1)} collective-permute-done((bf16[192,1536]{1,0:T(8,128)(2,1)S(1)}, bf16[192,1536]{1,0:T(8,128)(2,1)S(1)}, u32[]{:S(2)}, u32[]{:S(2)}) %collective-permute-start.6) | collective-permute-done | bytes 589856 | tf_op jit(solution)/shard_map/ppermute | solution.py:19
  305.3 10.5 %collective-permute-done.7 = bf16[192,1536]{1,0:T(8,128)(2,1)S(1)} collective-permute-done((bf16[192,1536]{1,0:T(8,128)(2,1)S(1)}, bf16[192,1536]{1,0:T(8,128)(2,1)S(1)}, u32[]{:S(2)}, u32[]{:S(2)}) %collective-permute-start.7) | collective-permute-done | bytes 589856 | tf_op jit(solution)/shard_map/ppermute | solution.py:19
  315.8 10.5 %collective-permute-done.8 = bf16[192,1536]{1,0:T(8,128)(2,1)S(1)} collective-permute-done((bf16[192,1536]{1,0:T(8,128)(2,1)S(1)}, bf16[192,1536]{1,0:T(8,128)(2,1)S(1)}, u32[]{:S(2)}, u32[]{:S(2)}) %collective-permute-start.8) | collective-permute-done | bytes 589856 | tf_op jit(solution)/shard_map/ppermute | solution.py:19
  326.3 10.6 %collective-permute-done.9 = bf16[192,1536]{1,0:T(8,128)(2,1)} collective-permute-done((bf16[192,1536]{1,0:T(8,128)(2,1)S(1)}, bf16[192,1536]{1,0:T(8,128)(2,1)}, u32[]{:S(2)}, u32[]{:S(2)}) %collective-permute-start.9) | collective-permute-done | bytes 589856 | tf_op jit(solution)/shard_map/ppermute | solution.py:19
  337.0 10.8 %collective-permute-done.10 = bf16[192,1536]{1,0:T(8,128)(2,1)} collective-permute-done((bf16[192,1536]{1,0:T(8,128)(2,1)}, bf16[192,1536]{1,0:T(8,128)(2,1)}, u32[]{:S(2)}, u32[]{:S(2)}) %collective-permute-start.10) | collective-permute-done | bytes 589856 | tf_op jit(solution)/shard_map/ppermute | solution.py:19
  347.8 5.0 %fusion.44 = (bf16[16,55296]{1,0:T(8,128)(2,1)}, bf16[16,55296]{1,0:T(8,128)(2,1)}, bf16[16,55296]{1,0:T(8,128)(2,1)}) fusion(bf16[16,362496]{1,0:T(8,128)(2,1)} %reshape.228), kind=kLoop, calls=%fused_computation.101 | loop fusion | bytes 10616832 | tf_op jit(solution)/shard_map/slice | solution.py:163
  352.7 4.8 %reshape.225 = bf16[576,1536]{1,0:T(8,128)(2,1)} reshape(bf16[16,55296]{1,0:T(8,128)(2,1)} %get-tuple-element.234) | data formatting | bytes 3538944 | tf_op jit(solution)/shard_map/reshape | solution.py:163
  357.5 4.8 %reshape.227 = bf16[576,1536]{1,0:T(8,128)(2,1)} reshape(bf16[16,55296]{1,0:T(8,128)(2,1)} %get-tuple-element.235) | data formatting | bytes 3538944 | tf_op jit(solution)/shard_map/reshape | solution.py:163
  362.3 4.8 %reshape.226 = bf16[576,1536]{1,0:T(8,128)(2,1)} reshape(bf16[16,55296]{1,0:T(8,128)(2,1)} %get-tuple-element.236) | data formatting | bytes 3538944 | tf_op jit(solution)/shard_map/reshape | solution.py:163
  368.2 1.1 constant_dynamic-update-slice_fusion.14
  369.3 1.1 constant_dynamic-update-slice_fusion.13
  370.8 1.1 constant_dynamic-update-slice_fusion.7
  371.9 1.1 constant_dynamic-update-slice_fusion.6
  373.0 1.2 constant_dynamic-update-slice_fusion.5
  374.7 3.7 copy-done.12
  378.4 4.7 %fusion.15 = f32[1536,576]{0,1:T(8,128)} fusion(bf16[576,1536]{1,0:T(8,128)(2,1)S(1)} %copy-done.3, bf16[3072,1536]{1,0:T(8,128)(2,1)S(1)} %constant_dynamic-update-slice_fusion, s32[]{:T(128)S(6)} %select_n.125), kind=kOutput, calls=%fused_computation.23 | convolution fusion | flops 2717908992 | bytes 10027012 | tf_op jit(solution)/shard_map/dot_general | solution.py:78
  383.1 13.9 %convolution_convert_fusion = bf16[1536,1536]{1,0:T(8,128)(2,1)} fusion(bf16[576,1536]{1,0:T(8,128)(2,1)} %reshape.227, f32[1536,576]{0,1:T(8,128)} %fusion.15, bf16[576,1536]{1,0:T(8,128)(2,1)} %reshape.225, bf16[3072,1536]{1,0:T(8,128)(2,1)} %copy-done.12, s32[]{:T(128)S(6)} %select_n.125), kind=kOutput, calls=%fused_computation.22 | convolution fusion | flops 5443485696 | bytes 16515076 | tf_op jit(solution)/shard_map/dot_general | solution.py:80
  398.8 37.0 %reduce-scatter.2.cloned.1.call-done = bf16[192,1536]{1,0:T(8,128)(2,1)} async-done(((bf16[1536,1536]{1,0:T(8,128)(2,1)}), bf16[192,1536]{1,0:T(8,128)(2,1)}) %reduce-scatter.2.cloned.1.call-update) | async-done | bytes 589840 | tf_op jit(solution)/shard_map/reduce_scatter | solution.py:194
  435.8 2.0 fusion.31
  (148 shorter events, 24.8 us)
Async XLA Ops:
  7.2 18.2 %copy-start = (bf16[1536,512]{1,0:T(8,128)(2,1)S(1)}, bf16[1536,512]{1,0:T(8,128)(2,1)}, u32[]{:S(2)}) copy-start(bf16[1536,512]{1,0:T(8,128)(2,1)} %param.19) | copy-start | bytes 4718596
  7.2 18.2 %copy-start.10 = (bf16[192,1536]{1,0:T(8,128)(2,1)S(1)}, bf16[192,1536]{1,0:T(8,128)(2,1)}, u32[]{:S(2)}) copy-start(bf16[192,1536]{1,0:T(8,128)(2,1)} %param.15) | copy-start | bytes 1769476
  7.2 18.2 %copy-start.15 = (f32[1536]{0:T(1024)S(1)}, f32[1536]{0:T(1024)}, u32[]{:S(2)}) copy-start(f32[1536]{0:T(1024)} %param.17) | copy-start | bytes 18436
  7.2 162.4 %all-gather.3.cloned.1.call-start = ((), (), s32[]{:S(2)}) async-start(), calls=%async_computation.2 | async-start | bytes 12324864 | tf_op jit(solution)/shard_map/all_gather | solution.py:158
  13.3 13.1 %collective-permute-start = (s32[3]{0:T(128)S(1)}, s32[3]{0:T(128)S(1)}, u32[]{:S(2)}, u32[]{:S(2)}) collective-permute-start(s32[3]{0:T(128)S(1)} %pad_add_fusion), channel_id=1, source_target_pairs={{0,1},{1,2},{2,3},{3,4},{4,5},{5,6},{6,7},{7,8},{8,9},{9,10},{10,1... | collective-permute-start | bytes 44 | tf_op jit(solution)/shard_map/ppermute | solution.py:103
  18.8 7.5 %copy-start.13 = (f32[64]{0:T(128)S(1)}, f32[64]{0:T(128)}, u32[]{:S(2)}) copy-start(f32[64]{0:T(128)} %param.22) | copy-start | bytes 772
  25.4 55.2 %copy-start.8 = (bf16[192,512]{1,0:T(8,128)(2,1)}, bf16[192,512]{1,0:T(8,128)(2,1)S(1)}, u32[]{:S(2)}) copy-start(bf16[192,512]{1,0:T(8,128)(2,1)S(1)} %convolution_convert_fusion.1) | copy-start | bytes 589828
  32.2 6.8 %collective-permute-start.1 = (s32[3]{0:T(128)S(1)}, s32[3]{0:T(128)S(1)}, u32[]{:S(2)}, u32[]{:S(2)}) collective-permute-start(s32[3]{0:T(128)S(1)} %broadcast_select_fusion), channel_id=1, source_target_pairs={{0,2},{1,3},{2,4},{3,5},{4,6},{5,7},{6,8},{7,9},{8,10},{9,11},{10,... | collective-permute-start | bytes 44 | tf_op jit(solution)/shard_map/ppermute | solution.py:103
  45.4 5.7 %collective-permute-start.2 = (s32[3]{0:T(128)S(1)}, s32[3]{0:T(128)S(1)}, u32[]{:S(2)}, u32[]{:S(2)}) collective-permute-start(s32[3]{0:T(128)S(1)} %broadcast_select_fusion.1), channel_id=1, source_target_pairs={{0,4},{1,5},{2,6},{3,7},{4,8},{5,9},{6,10},{7,11},{8,12},{9,13},{1... | collective-permute-start | bytes 44 | tf_op jit(solution)/shard_map/ppermute | solution.py:103
  58.4 7.0 %collective-permute-start.3 = (s32[3]{0:T(128)S(1)}, s32[3]{0:T(128)S(1)}, u32[]{:S(2)}, u32[]{:S(2)}) collective-permute-start(s32[3]{0:T(128)S(1)} %broadcast_select_fusion.2), channel_id=1, source_target_pairs={{0,8},{1,9},{2,10},{3,11},{4,12},{5,13},{6,14},{7,15},{16,24},{17,... | collective-permute-start | bytes 44 | tf_op jit(solution)/shard_map/ppermute | solution.py:103
  72.5 5.1 %collective-permute-start.4 = (s32[3]{0:T(128)S(1)}, s32[3]{0:T(128)S(1)}, u32[]{:S(2)}, u32[]{:S(2)}) collective-permute-start(s32[3]{0:T(128)S(1)} %broadcast_select_fusion.3), channel_id=1, source_target_pairs={{0,1},{1,2},{2,3},{3,4},{4,5},{5,6},{6,7},{7,8},{8,9},{9,10},{10,1... | collective-permute-start | bytes 44 | tf_op jit(solution)/shard_map/ppermute | solution.py:109
  80.6 5.5 %copy-start.4 = (bf16[192,512]{1,0:T(8,128)(2,1)}, bf16[192,512]{1,0:T(8,128)(2,1)S(1)}, u32[]{:S(2)}) copy-start(bf16[192,512]{1,0:T(8,128)(2,1)S(1)} %copy.23) | copy-start | bytes 589828
  81.7 354.2 %reduce-scatter.2.cloned.1.call-start = ((), (), s32[]{:S(2)}) async-start(), calls=%async_computation.1 | async-start | bytes 5308416 | tf_op jit(solution)/shard_map/reduce_scatter | solution.py:194
  81.7 4.6 %copy-start.14 = (f32[64]{0:T(128)S(1)}, f32[64]{0:T(128)}, u32[]{:S(2)}) copy-start(f32[64]{0:T(128)} %param.21) | copy-start | bytes 772
  208.6 5.3 %copy-start.2 = (f32[8,768,3,192]{1,3,2,0:T(8,128)}, f32[8,768,3,192]{1,3,2,0:T(8,128)S(1)}, u32[]{:S(2)}) copy-start(f32[8,768,3,192]{1,3,2,0:T(8,128)S(1)} %get-tuple-element.337) | copy-start | bytes 42467332 | tf_op jit(solution)/shard_map/while
  208.7 5.3 %copy-start.6 = (f32[8,3,192,64]{2,3,1,0:T(8,128)S(1)}, f32[8,3,192,64]{2,3,1,0:T(8,128)}, u32[]{:S(2)}) copy-start(f32[8,3,192,64]{2,3,1,0:T(8,128)} %get-tuple-element.357) | copy-start | bytes 3538948 | tf_op jit(solution)/shard_map/while
  221.1 1.2 copy-start.7
  227.4 5.3 %copy-start.2 = (f32[8,768,3,192]{1,3,2,0:T(8,128)}, f32[8,768,3,192]{1,3,2,0:T(8,128)S(1)}, u32[]{:S(2)}) copy-start(f32[8,768,3,192]{1,3,2,0:T(8,128)S(1)} %get-tuple-element.337) | copy-start | bytes 42467332 | tf_op jit(solution)/shard_map/while
  227.5 5.3 %copy-start.6 = (f32[8,3,192,64]{2,3,1,0:T(8,128)S(1)}, f32[8,3,192,64]{2,3,1,0:T(8,128)}, u32[]{:S(2)}) copy-start(f32[8,3,192,64]{2,3,1,0:T(8,128)} %get-tuple-element.357) | copy-start | bytes 3538948 | tf_op jit(solution)/shard_map/while
  239.9 1.2 copy-start.7
  246.2 5.3 %copy-start.2 = (f32[8,768,3,192]{1,3,2,0:T(8,128)}, f32[8,768,3,192]{1,3,2,0:T(8,128)S(1)}, u32[]{:S(2)}) copy-start(f32[8,768,3,192]{1,3,2,0:T(8,128)S(1)} %get-tuple-element.337) | copy-start | bytes 42467332 | tf_op jit(solution)/shard_map/while
  246.3 5.3 %copy-start.6 = (f32[8,3,192,64]{2,3,1,0:T(8,128)S(1)}, f32[8,3,192,64]{2,3,1,0:T(8,128)}, u32[]{:S(2)}) copy-start(f32[8,3,192,64]{2,3,1,0:T(8,128)} %get-tuple-element.357) | copy-start | bytes 3538948 | tf_op jit(solution)/shard_map/while
  258.6 1.2 copy-start.7
  265.0 5.3 %copy-start.2 = (f32[8,768,3,192]{1,3,2,0:T(8,128)}, f32[8,768,3,192]{1,3,2,0:T(8,128)S(1)}, u32[]{:S(2)}) copy-start(f32[8,768,3,192]{1,3,2,0:T(8,128)S(1)} %get-tuple-element.337) | copy-start | bytes 42467332 | tf_op jit(solution)/shard_map/while
  265.0 5.3 %copy-start.6 = (f32[8,3,192,64]{2,3,1,0:T(8,128)S(1)}, f32[8,3,192,64]{2,3,1,0:T(8,128)}, u32[]{:S(2)}) copy-start(f32[8,3,192,64]{2,3,1,0:T(8,128)} %get-tuple-element.357) | copy-start | bytes 3538948 | tf_op jit(solution)/shard_map/while
  277.4 1.2 copy-start.7
  280.2 3.8 copy-start.11
  284.2 10.5 %collective-permute-start.5 = (bf16[192,1536]{1,0:T(8,128)(2,1)S(1)}, bf16[192,1536]{1,0:T(8,128)(2,1)S(1)}, u32[]{:S(2)}, u32[]{:S(2)}) collective-permute-start(bf16[192,1536]{1,0:T(8,128)(2,1)S(1)} %fusion.30), channel_id=1, source_target_pairs={{0,16},{16,32},{32,48},{48,64},{64,80},{80,96},{96,112},{112,0},{1... | collective-permute-start | bytes 1769480 | tf_op jit(solution)/shard_map/ppermute | solution.py:19
  294.8 10.5 %collective-permute-start.6 = (bf16[192,1536]{1,0:T(8,128)(2,1)S(1)}, bf16[192,1536]{1,0:T(8,128)(2,1)S(1)}, u32[]{:S(2)}, u32[]{:S(2)}) collective-permute-start(bf16[192,1536]{1,0:T(8,128)(2,1)S(1)} %collective-permute-done.5), channel_id=1, source_target_pairs={{0,16},{16,32},{32,48},{48,64},{64,80},{80,96},{96,112},{112,0},{1... | collective-permute-start | bytes 1769480 | tf_op jit(solution)/shard_map/ppermute | solution.py:19
  305.3 10.5 %collective-permute-start.7 = (bf16[192,1536]{1,0:T(8,128)(2,1)S(1)}, bf16[192,1536]{1,0:T(8,128)(2,1)S(1)}, u32[]{:S(2)}, u32[]{:S(2)}) collective-permute-start(bf16[192,1536]{1,0:T(8,128)(2,1)S(1)} %collective-permute-done.6), channel_id=1, source_target_pairs={{0,16},{16,32},{32,48},{48,64},{64,80},{80,96},{96,112},{112,0},{1... | collective-permute-start | bytes 1769480 | tf_op jit(solution)/shard_map/ppermute | solution.py:19
  315.8 10.5 %collective-permute-start.8 = (bf16[192,1536]{1,0:T(8,128)(2,1)S(1)}, bf16[192,1536]{1,0:T(8,128)(2,1)S(1)}, u32[]{:S(2)}, u32[]{:S(2)}) collective-permute-start(bf16[192,1536]{1,0:T(8,128)(2,1)S(1)} %collective-permute-done.7), channel_id=1, source_target_pairs={{0,16},{16,32},{32,48},{48,64},{64,80},{80,96},{96,112},{112,0},{1... | collective-permute-start | bytes 1769480 | tf_op jit(solution)/shard_map/ppermute | solution.py:19
  326.3 10.6 %collective-permute-start.9 = (bf16[192,1536]{1,0:T(8,128)(2,1)S(1)}, bf16[192,1536]{1,0:T(8,128)(2,1)}, u32[]{:S(2)}, u32[]{:S(2)}) collective-permute-start(bf16[192,1536]{1,0:T(8,128)(2,1)S(1)} %collective-permute-done.8), channel_id=1, source_target_pairs={{0,16},{16,32},{32,48},{48,64},{64,80},{80,96},{96,112},{112,0},{1... | collective-permute-start | bytes 1769480 | tf_op jit(solution)/shard_map/ppermute | solution.py:19
  336.9 10.8 %collective-permute-start.10 = (bf16[192,1536]{1,0:T(8,128)(2,1)}, bf16[192,1536]{1,0:T(8,128)(2,1)}, u32[]{:S(2)}, u32[]{:S(2)}) collective-permute-start(bf16[192,1536]{1,0:T(8,128)(2,1)} %collective-permute-done.9), channel_id=1, source_target_pairs={{0,16},{16,32},{32,48},{48,64},{64,80},{80,96},{96,112},{112,0},{1... | collective-permute-start | bytes 1769480 | tf_op jit(solution)/shard_map/ppermute | solution.py:19
  347.8 19.3 %collective-permute-start.11 = (bf16[192,1536]{1,0:T(8,128)(2,1)}, bf16[192,1536]{1,0:T(8,128)(2,1)}, u32[]{:S(2)}, u32[]{:S(2)}) collective-permute-start(bf16[192,1536]{1,0:T(8,128)(2,1)} %collective-permute-done.10), channel_id=1, source_target_pairs={{0,16},{16,32},{32,48},{48,64},{64,80},{80,96},{96,112},{112,0},{1... | collective-permute-start | bytes 1769480 | tf_op jit(solution)/shard_map/ppermute | solution.py:19
  373.0 5.3 %copy-start.3 = (bf16[576,1536]{1,0:T(8,128)(2,1)S(1)}, bf16[576,1536]{1,0:T(8,128)(2,1)}, u32[]{:S(2)}) copy-start(bf16[576,1536]{1,0:T(8,128)(2,1)} %reshape.226) | copy-start | bytes 5308420
  374.7 3.7 copy-start.12
  397.0 0.9 copy-start.5
  397.0 1.0 copy-start.9
  397.0 40.9 %copy-start.1 = (bf16[1536,512]{1,0:T(8,128)(2,1)S(1)}, bf16[1536,512]{1,0:T(8,128)(2,1)}, u32[]{:S(2)}) copy-start(bf16[1536,512]{1,0:T(8,128)(2,1)} %param.19) | copy-start | bytes 4718596
Sparse Core Ops, SparseCore 0:
  81.8 87.7 all-gather.2
  397.2 38.6 reduce-scatter.1
